TPU v7x, 256 devices: a whole 4x4x8 slice. The times are simulated.
256 devices in a mesh: ctx: 32 (over x, z), head: 8 (over y, core).
Axes of the slice: x: 4, y: 4, z: 8, core: 2. Of those that a mesh axis runs over, the one named last changes fastest.
Arguments:
- features: bfloat16 [8192, 16384], P('ctx', 'head'), may hold values from -6 to 6
- log_decay: float32 [256, 8192], P('head', 'ctx'), may hold values from -2 to 0, as said below
- step_size: float32 [256, 8192], P('head', 'ctx'), may hold values from 0.0002 to 0.002
- b_matrix: bfloat16 [8192, 2048], P('ctx', 'head'), may hold values from -6 to 6
- c_matrix: bfloat16 [8192, 2048], P('ctx', 'head'), may hold values from -6 to 6
- skip_gain: float32 [256], P('head'), may hold values from 0.5 to 1.5
Outputs:
- mixed: bfloat16 [8192, 16384], P('ctx', 'head')
Inputs may be any that keep to these rules, and one draw needn't show every extreme that they name: `log_decay`: every entry is negative.
All inputs are finite; a program needn't handle non-finite values.
Results may differ from a plain program's by a relative error of at most 0.0013.
Values sent between devices are 32-bit elements; how exact they have to be, the bound alone decides.
No kernel may reach another device: no remote copies, remote signals or barrier semaphores. Data moves between devices by JAX's collectives and lax.ppermute only.
A program may use at most 320 MiB of HBM per device.

v0:
```python
import jax
import jax.numpy as jnp
import numpy as np
from jax import lax
from jax.sharding import PartitionSpec as P

N = 256
SPAN = 128


def chain_mixing(decay, devices, halves):
    j = np.arange(devices)
    pos = np.stack([j, halves * devices - 1 - j], axis=1).reshape(-1)
    between = (pos[None, :, None] < pos[None, None, :]) & (pos[None, None, :] < pos[:, None, None])
    gap = jnp.sum(jnp.where(between[None], decay[:, None, None, :], 0.0), axis=-1)
    lower = pos[None, :] < pos[:, None]
    mixing = jnp.where(lower[None], jnp.exp(gap), 0.0)
    return mixing.reshape(-1, devices, halves, devices, halves)


def on_device(features, log_decay, step_size, b_matrix, c_matrix, skip_gain):
    head_count = log_decay.shape[0]
    tok_rows = features.shape[0]
    head_width = features.shape[1] // head_count
    state_size = N
    group_count = b_matrix.shape[1] // state_size
    per_group = head_count // group_count
    halves = tok_rows // SPAN
    assert halves == 2
    devices = lax.axis_size("ctx")
    per_chunk = head_count // devices
    flat = head_width * state_size
    rows = halves * head_width
    extra = 8
    cumulative = jnp.cumsum(log_decay.reshape(head_count, halves, SPAN), axis=2)
    totals = cumulative[:, :, -1]
    step_rows = step_size.reshape(head_count, halves, SPAN)
    grouped_inputs = features.reshape(halves, SPAN, group_count, per_group, head_width)
    b_spans = b_matrix.reshape(halves, SPAN, group_count, state_size)
    c_spans = c_matrix.reshape(halves, SPAN, group_count, state_size)
    coeffs = jnp.exp(totals[:, :, None] - cumulative) * step_rows
    coeffs = jnp.transpose(coeffs.reshape(group_count, per_group, halves, SPAN), (2, 3, 0, 1))
    weighted = (grouped_inputs * coeffs[..., None]).astype(jnp.bfloat16)
    span_states = jnp.einsum(
        "ksgn,ksgqp->gqkpn", b_spans, weighted, preferred_element_type=jnp.float32
    ).reshape(head_count, rows, state_size)
    me = lax.axis_index("ctx")
    spread = jnp.zeros((devices, halves, head_count), jnp.float32)
    spread = lax.dynamic_update_slice_in_dim(spread, jnp.transpose(totals)[None], me, axis=0)
    all_decay = lax.psum(spread, "ctx")
    got = lax.all_to_all(span_states, "ctx", 0, 0, tiled=True)
    got_states = got.reshape(devices, per_chunk, halves, head_width, state_size)
    mine = lax.dynamic_slice_in_dim(all_decay, me * per_chunk, per_chunk, axis=2)
    mixing = chain_mixing(
        jnp.transpose(mine, (2, 0, 1)).reshape(per_chunk, devices * halves), devices, halves
    )
    j = np.arange(devices)
    own = np.zeros((devices, halves, devices, halves), bool)
    own[j, 1, j, 0] = True
    others = jnp.where(own[None], 0.0, mixing)
    if per_chunk == 1:
        solved = jnp.einsum(
            "uv,vpn->upn",
            others.reshape(devices * halves, devices * halves),
            got.reshape(devices * halves, head_width, state_size),
            precision=lax.Precision.HIGHEST,
            preferred_element_type=jnp.float32,
        ).reshape(devices, rows, state_size)
    else:
        solved = jnp.einsum(
            "cjkJL,JcLpn->jckpn",
            others,
            got_states,
            precision=lax.Precision.HIGHEST,
            preferred_element_type=jnp.float32,
        ).reshape(devices * per_chunk, rows, state_size)
    back = lax.all_to_all(solved, "ctx", 0, 0, tiled=True)
    later = np.arange(devices)[:, None] > me
    gain = jnp.exp(jnp.sum(jnp.where(later, jnp.sum(all_decay, axis=1), 0.0), axis=0))
    state_halves = [
        back[:, :head_width].astype(jnp.bfloat16).reshape(head_count * head_width, state_size),
        (back[:, head_width:rows] + gain[:, None, None] * span_states[:, :head_width])
        .astype(jnp.bfloat16)
        .reshape(head_count * head_width, state_size),
    ]
    scores = jnp.einsum("ktgn,ksgn->gkts", c_spans, b_spans, preferred_element_type=jnp.float32)
    causal = jnp.arange(SPAN)[:, None] >= jnp.arange(SPAN)[None, :]
    cum_grouped = cumulative.reshape(group_count, per_group, halves, SPAN)
    step_grouped = step_rows.reshape(group_count, per_group, halves, SPAN)
    decay_gaps = jnp.where(causal, cum_grouped[..., :, None] - cum_grouped[..., None, :], -jnp.inf)
    weights = (scores[:, None] * jnp.exp(decay_gaps) * step_grouped[:, :, :, None, :]).astype(
        jnp.bfloat16
    )
    diagonal_part = jnp.einsum(
        "gqkts,ksgqp->ktgqp", weights, grouped_inputs, preferred_element_type=jnp.float32
    ).reshape(halves, SPAN, head_count * head_width)
    decay_in = jnp.repeat(jnp.transpose(jnp.exp(cumulative), (1, 2, 0)), head_width, axis=2)
    skip = jnp.repeat(skip_gain, head_width)[None, :]
    inputs = features.reshape(halves, SPAN, head_count * head_width).astype(jnp.float32)
    per_group_width = per_group * head_width
    outs = []
    for k in range(halves):
        state_part = jnp.concatenate(
            [
                jnp.dot(
                    c_spans[k, :, g],
                    state_halves[k][g * per_group_width : (g + 1) * per_group_width].T,
                    preferred_element_type=jnp.float32,
                )
                for g in range(group_count)
            ],
            axis=1,
        )
        outs.append(diagonal_part[k] + state_part * decay_in[k] + skip * inputs[k])
    return jnp.concatenate(outs, axis=0).astype(jnp.bfloat16)


def solution(mesh):
    placed = (
        P("ctx", "head"),
        P("head", "ctx"),
        P("head", "ctx"),
        P("ctx", "head"),
        P("ctx", "head"),
        P("head"),
    )
    return jax.shard_map(
        on_device, mesh=mesh, in_specs=placed, out_specs=P("ctx", "head"), check_vma=False
    )
```

profile of v0, /device:TPU:16, one launch (start us, length us, event | category | flops | bytes accessed | tf_op | source)
XLA Modules:
  0.0 344.3 jit_solution(12947823522675433255)
XLA Ops:
  0.0 0.0 copy-start
  0.0 0.8 copy_bitcast_fusion.1
  0.8 0.6 reduce_window_sum.13
  1.4 0.2 slice_reduce_fusion
  1.5 0.8 reshape.145
  2.3 0.1 fusion.26
  2.4 1.5 copy.52
  3.9 0.3 reshape.142
  4.2 0.0 copy-start.2
  4.2 1.1 multiply_convert_fusion.2
  5.3 0.0 copy-done
  5.3 0.7 convolution_bitcast_fusion.2
  6.0 2.2 copy.58
  8.2 0.0 copy-done.2
  8.3 11.6 %all-to-all-start = ((f32[32,128,256]{2,1,0:T(8,128)}), f32[32,128,256]{2,1,0:T(8,128)}, u32[]{:S(2)}, u32[]{:S(2)}) async-start(f32[32,128,256]{2,1,0:T(8,128)} %bitcast.92), calls=%async_computation | async-start | bytes 8388608 | tf_op jit(solution)/shard_map/all_to_all | solution.py:51
  19.9 0.1 copy.54
  20.0 0.1 dynamic_update_slice.3
  20.1 232.9 %psum.7 = f32[32,2,32]{1,0,2:T(8,128)S(1)} all-reduce(f32[32,2,32]{1,0,2:T(8,128)S(1)} %dynamic_update_slice.3), channel_id=1, replica_groups=mesh['ctx'=32,'head'=8] {'ctx'}, use_global_device_ids=true, to_apply=%region_1.2 | all-reduce | flops 2048 | bytes 16384 | tf_op jit(solution)/shard_map/psum | solution.py:50
  253.0 0.1 broadcast_in_dim.72
  253.1 0.0 copy-done.8
  253.1 0.6 select_reduce_fusion
  253.7 0.0 all-to-all-done
  253.8 8.4 %fusion = f32[64,64,256]{2,0,1:T(8,128)S(1)} fusion(f32[64,64,256]{2,1,0:T(8,128)} %bitcast.17, pred[64,64]{1,0:T(32,128)(4,1)S(1)} %copy-done.11, pred[64,64]{1,0:T(32,128)(4,1)S(1)} %copy-done.10, f32[64,64]{1,0:T(8,128)S(1)} %select_reduce_fusion), kind=kOutput, calls=%fused_computation | convolution fusion | flops 805314560 | bytes 8413184 | tf_op jit(solution)/shard_map/uv,vpn->upn/dot_general | solution.py:62
  262.2 4.4 %copy.60 = f32[64,64,256]{2,1,0:T(8,128)} copy(f32[64,64,256]{2,0,1:T(8,128)S(1)} %fusion) | data formatting | bytes 8388608 | tf_op jit(solution)/shard_map/uv,vpn->upn/dot_general | solution.py:62
  266.6 5.2 %all-to-all-start.1 = ((f32[32,128,256]{2,1,0:T(8,128)}), f32[32,128,256]{2,1,0:T(8,128)}, u32[]{:S(2)}, u32[]{:S(2)}) async-start(f32[32,128,256]{2,1,0:T(8,128)} %bitcast.94), calls=%async_computation.1 | async-start | bytes 8388608 | tf_op jit(solution)/shard_map/all_to_all | solution.py:77
  271.8 0.2 reduce_sum.28
  272.0 0.0 copy-done.1
  272.0 0.2 convert_element_type.30
  272.3 0.1 select_reduce_fusion.1
  272.4 0.2 fusion.35
  272.6 3.6 %fusion.19 = f32[2,128,1,32,64]{1,4,3,0,2:T(8,128)S(1)} fusion(f32[32,2,128]{2,0,1:T(8,128)S(1)} %copy_bitcast_fusion, f32[32,2,128]{2,0,1:T(8,128)S(1)} %reduce_window_sum.13, f32[2,128,128]{2,1,0:T(8,128)S(1)} %fusion.35, pred[128,128]{1,0:T(8,128)(4,1)S(1)} %iota_compare_fusion, bf16[2,128,32,64]{1,0,3,2:T(2,128)(2,1)} %copy-done.2), kind=kOutput, calls=%fused_computation.27 | convolution fusion | flops 139460608 | bytes 3358720 | tf_op jit(solution)/shard_map/gqkts,ksgqp->ktgqp/dot_general | solution.py:94
  276.2 0.0 copy-start.12
  276.2 1.2 fusion.34
  277.4 1.3 copy.64
  278.7 0.1 broadcast_in_dim.82
  278.8 1.3 copy.63
  280.2 0.1 broadcast_in_dim.78
  280.2 0.1 mul.87
  280.3 2.6 copy.62
  282.9 0.1 broadcast_in_dim.76
  283.0 1.3 copy.61
  284.3 53.5 %all-to-all-done.1 = f32[32,128,256]{2,1,0:T(8,128)} async-done(((f32[32,128,256]{2,1,0:T(8,128)}), f32[32,128,256]{2,1,0:T(8,128)}, u32[]{:S(2)}, u32[]{:S(2)}) %all-to-all-start.1) | async-done | bytes 4194336 | tf_op jit(solution)/shard_map/all_to_all | solution.py:77
  337.8 2.6 fusion.12
  340.4 0.0 copy-start.6
  340.4 0.5 fusion.8
  340.9 1.8 slice.95
  342.7 0.5 fusion.9
  343.3 1.1 pad_maximum_fusion
  (29 shorter events, 0.2 us)
Async XLA Ops:
  0.0 5.3 %copy-start = (bf16[256,256]{1,0:T(8,128)(2,1)S(1)}, bf16[256,256]{1,0:T(8,128)(2,1)}, u32[]{:S(2)}) copy-start(bf16[256,256]{1,0:T(8,128)(2,1)} %param.13) | copy-start | bytes 393220
  4.2 4.0 %copy-start.2 = (bf16[2,128,32,64]{1,0,3,2:T(2,128)(2,1)}, bf16[2,128,32,64]{1,0,3,2:T(2,128)(2,1)S(1)}, u32[]{:S(2)}) copy-start(bf16[2,128,32,64]{1,0,3,2:T(2,128)(2,1)S(1)} %reshape.142) | copy-start | bytes 3145732
  8.3 244.9 %copy-start.8 = (pred[1,64,64,64]{3,2,1,0:T(32,128)(4,1)S(1)}, pred[1,64,64,64]{3,2,1,0:T(32,128)(4,1)}, u32[]{:S(2)}) copy-start(pred[1,64,64,64]{3,2,1,0:T(32,128)(4,1)} %constant.26.clone) | copy-start | bytes 786436
  8.3 245.5 %copy-start.10 = (pred[64,64]{1,0:T(32,128)(4,1)S(1)}, pred[64,64]{1,0:T(32,128)(4,1)}, u32[]{:S(2)}) copy-start(pred[64,64]{1,0:T(32,128)(4,1)} %constant.31) | copy-start | bytes 12292
  8.3 245.5 %copy-start.11 = (pred[64,64]{1,0:T(32,128)(4,1)S(1)}, pred[64,64]{1,0:T(32,128)(4,1)}, u32[]{:S(2)}) copy-start(pred[64,64]{1,0:T(32,128)(4,1)} %constant.32) | copy-start | bytes 12292
  8.3 245.5 %all-to-all-start = ((f32[32,128,256]{2,1,0:T(8,128)}), f32[32,128,256]{2,1,0:T(8,128)}, u32[]{:S(2)}, u32[]{:S(2)}) async-start(f32[32,128,256]{2,1,0:T(8,128)} %bitcast.92), calls=%async_computation | async-start | bytes 8388608 | tf_op jit(solution)/shard_map/all_to_all | solution.py:51
  266.6 5.4 %copy-start.1 = (bf16[256,2048]{1,0:T(8,128)(2,1)S(1)}, bf16[256,2048]{1,0:T(8,128)(2,1)}, u32[]{:S(2)}) copy-start(bf16[256,2048]{1,0:T(8,128)(2,1)} %param.10) | copy-start | bytes 3145732
  266.6 5.7 %copy-start.13 = (s32[32,1]{0,1:T(1,128)S(1)}, s32[32,1]{0,1:T(1,128)}, u32[]{:S(2)}) copy-start(s32[32,1]{0,1:T(1,128)} %constant.29.clone) | copy-start | bytes 388
  266.6 5.8 %copy-start.9 = (f32[32,256]{1,0:T(8,128)S(1)}, f32[32,256]{1,0:T(8,128)}, u32[]{:S(2)}) copy-start(f32[32,256]{1,0:T(8,128)} %param.12) | copy-start | bytes 98308
  266.6 5.9 %copy-start.7 = (bf16[256,256]{1,0:T(8,128)(2,1)S(1)}, bf16[256,256]{1,0:T(8,128)(2,1)}, u32[]{:S(2)}) copy-start(bf16[256,256]{1,0:T(8,128)(2,1)} %param.14) | copy-start | bytes 393220
  266.6 71.2 %all-to-all-start.1 = ((f32[32,128,256]{2,1,0:T(8,128)}), f32[32,128,256]{2,1,0:T(8,128)}, u32[]{:S(2)}, u32[]{:S(2)}) async-start(f32[32,128,256]{2,1,0:T(8,128)} %bitcast.94), calls=%async_computation.1 | async-start | bytes 8388608 | tf_op jit(solution)/shard_map/all_to_all | solution.py:77
  276.2 3.9 %copy-start.12 = (f32[32]{0:T(128)S(1)}, f32[32]{0:T(128)}, u32[]{:S(2)}) copy-start(f32[32]{0:T(128)} %param.15) | copy-start | bytes 388
  284.3 56.1 %copy-start.3 = (f32[128,2048]{1,0:T(8,128)S(1)}, f32[128,2048]{1,0:T(8,128)}, u32[]{:S(2)}) copy-start(f32[128,2048]{1,0:T(8,128)} %copy.64) | copy-start | bytes 3145732
  337.8 2.6 copy-start.5
  340.4 2.4 copy-start.4
  340.4 2.4 copy-start.6
where the time goes:
time: 345 us; the launch traced here: 344 us
  blocking collectives  233 us (68%)
  waiting for transfers between devices  53.5 us (16%)
  local copies, waits for them, and re-layouts  20.4 us (6%)
  starting transfers between devices  16.8 us (5%)
  matrix products  13.9 us (4%)
  other arithmetic  6.54 us (2%)
    psum x1, blocking collectives, on_device(): all_decay = lax.psum(spread, 'ctx')  233 us
    all_to_all x1, waiting for transfers between devices, on_device(): back = lax.all_to_all(solved, 'ctx', 0, 0, tiled=True)  53.5 us
    all_to_all x1, starting transfers between devices, on_device(): got = lax.all_to_all(span_states, 'ctx', 0, 0, tiled=True)  11.6 us
    dot_general x1, matrix products, on_device(): jnp.einsum('uv,vpn->upn', others.reshape(devices * halves, devices * halv...  8.4 us
  transfers between devices with their start and end apart: 2, of which 1 were waited for; matrix products, arithmetic and copies ran while one was open for 4% of the time, Pallas kernels for 0%

commit v1 on v0

--- a/solution.py
+++ b/solution.py
@@ -47,7 +47,11 @@
     me = lax.axis_index("ctx")
     spread = jnp.zeros((devices, halves, head_count), jnp.float32)
     spread = lax.dynamic_update_slice_in_dim(spread, jnp.transpose(totals)[None], me, axis=0)
-    all_decay = lax.psum(spread, "ctx")
+    all_decay = spread
+    for hop in (1, 2, 4, 8, 16):
+        all_decay = all_decay + lax.ppermute(
+            all_decay, "ctx", [(dev, dev ^ hop) for dev in range(32)]
+        )
     got = lax.all_to_all(span_states, "ctx", 0, 0, tiled=True)
     got_states = got.reshape(devices, per_chunk, halves, head_width, state_size)
     mine = lax.dynamic_slice_in_dim(all_decay, me * per_chunk, per_chunk, axis=2)

time: 345 us -> 259 us (0.75)
  blocking collectives: 233 us -> 0 us
  waiting for transfers between devices: 53.5 us -> 181 us
  starting transfers between devices: 16.8 us -> 35.8 us
    psum x1 -> x0, blocking collectives: 233 us -> none  [on_device(): all_decay = lax.psum(spread, 'ctx')]
    ppermute x0 -> x5, waiting for transfers between devices: none -> 101 us  [on_device(): lax.ppermute(all_decay, 'ctx', [(dev, dev ^ hop) for dev in range(32)])]
    all_to_all x1, waiting for transfers between devices: 53.5 us -> 80 us  [on_device(): back = lax.all_to_all(solved, 'ctx', 0, 0, tiled=True)]
    ppermute x0 -> x5, starting transfers between devices: none -> 14.3 us  [on_device(): lax.ppermute(all_decay, 'ctx', [(dev, dev ^ hop) for dev in range(32)])]
    all_to_all x1, starting transfers between devices: 5.18 us -> 9.87 us  [on_device(): back = lax.all_to_all(solved, 'ctx', 0, 0, tiled=True)]
  transfers between devices with their start and end apart: 2 -> 7, of which waited for: 1 -> 6; matrix products, arithmetic and copies ran while one was open for 4% -> 5% of each run, Pallas kernels for 0% -> 0%
where the time goes in v1:
time: 259 us
  waiting for transfers between devices  181 us (70%)
  starting transfers between devices  35.8 us (14%)
  local copies, waits for them, and re-layouts  20.5 us (8%)
  matrix products  15.5 us (6%)
  other arithmetic  5.77 us (2%)
    ppermute x5, waiting for transfers between devices, on_device(): lax.ppermute(all_decay, 'ctx', [(dev, dev ^ hop) for dev in range(32)])  101 us
    all_to_all x1, waiting for transfers between devices, on_device(): back = lax.all_to_all(solved, 'ctx', 0, 0, tiled=True)  80 us
    ppermute x5, starting transfers between devices, on_device(): lax.ppermute(all_decay, 'ctx', [(dev, dev ^ hop) for dev in range(32)])  14.3 us
    all_to_all x1, starting transfers between devices, on_device(): got = lax.all_to_all(span_states, 'ctx', 0, 0, tiled=True)  11.6 us
    all_to_all x1, starting transfers between devices, on_device(): back = lax.all_to_all(solved, 'ctx', 0, 0, tiled=True)  9.87 us
    dot_general x1, matrix products, on_device(): jnp.einsum('uv,vpn->upn', others.reshape(devices * halves, devices * halv...  8.4 us
  transfers between devices with their start and end apart: 7, of which 6 were waited for; matrix products, arithmetic and copies ran while one was open for 5% of the time, Pallas kernels for 0%

profile of v1, /device:TPU:16, one launch (start us, length us, event | category | flops | bytes accessed | tf_op | source)
XLA Modules:
  0.0 258.7 jit_solution(16041188850117148242)
XLA Ops:
  0.0 0.8 copy_bitcast_fusion.1
  0.8 0.6 reduce_window_sum.13
  1.4 0.2 slice_reduce_fusion
  1.5 0.8 reshape.145
  2.3 0.1 fusion.26
  2.4 1.5 copy.35
  3.9 0.3 reshape.142
  4.2 1.1 multiply_convert_fusion.2
  5.3 0.7 convolution_bitcast_fusion.2
  6.0 2.2 copy.40
  8.3 11.6 %all-to-all-start = ((f32[32,128,256]{2,1,0:T(8,128)}), f32[32,128,256]{2,1,0:T(8,128)}, u32[]{:S(2)}, u32[]{:S(2)}) async-start(f32[32,128,256]{2,1,0:T(8,128)} %bitcast.94), calls=%async_computation | async-start | bytes 8388608 | tf_op jit(solution)/shard_map/all_to_all | solution.py:55
  19.9 1.8 collective-permute-start
  21.7 89.6 %collective-permute-done = f32[32,2,32]{2,1,0:T(2,128)S(1)} collective-permute-done((f32[32,2,32]{2,1,0:T(2,128)S(1)}, f32[32,2,32]{2,1,0:T(2,128)S(1)}, u32[]{:S(2)}, u32[]{:S(2)}) %collective-permute-start) | collective-permute-done | bytes 8224 | tf_op jit(solution)/shard_map/ppermute | solution.py:52
  111.3 3.5 %collective-permute-start.1 = (f32[32,2,32]{2,1,0:T(2,128)S(1)}, f32[32,2,32]{2,1,0:T(2,128)S(1)}, u32[]{:S(2)}, u32[]{:S(2)}) collective-permute-start(f32[32,2,32]{2,1,0:T(2,128)S(1)} %fusion.32), channel_id=1, source_target_pairs={{0,16},{8,24},{16,0},{24,8},{32,48},{40,56},{48,32},{56,40},{64,80... | collective-permute-start | bytes 24584 | tf_op jit(solution)/shard_map/ppermute | solution.py:52
  114.9 2.2 collective-permute-done.1
  117.1 4.6 %collective-permute-start.2 = (f32[32,2,32]{2,1,0:T(2,128)S(1)}, f32[32,2,32]{2,1,0:T(2,128)S(1)}, u32[]{:S(2)}, u32[]{:S(2)}) collective-permute-start(f32[32,2,32]{2,1,0:T(2,128)S(1)} %add.37), channel_id=1, source_target_pairs={{0,32},{8,40},{16,48},{24,56},{32,0},{40,8},{48,16},{56,24},{64,96... | collective-permute-start | bytes 24584 | tf_op jit(solution)/shard_map/ppermute | solution.py:52
  121.8 3.3 %collective-permute-done.2 = f32[32,2,32]{2,1,0:T(2,128)S(1)} collective-permute-done((f32[32,2,32]{2,1,0:T(2,128)S(1)}, f32[32,2,32]{2,1,0:T(2,128)S(1)}, u32[]{:S(2)}, u32[]{:S(2)}) %collective-permute-start.2) | collective-permute-done | bytes 8224 | tf_op jit(solution)/shard_map/ppermute | solution.py:52
  125.1 1.5 collective-permute-start.3
  126.6 2.8 %collective-permute-done.3 = f32[32,2,32]{2,1,0:T(2,128)S(1)} collective-permute-done((f32[32,2,32]{2,1,0:T(2,128)S(1)}, f32[32,2,32]{2,1,0:T(2,128)S(1)}, u32[]{:S(2)}, u32[]{:S(2)}) %collective-permute-start.3) | collective-permute-done | bytes 8224 | tf_op jit(solution)/shard_map/ppermute | solution.py:52
  129.4 2.8 %collective-permute-start.4 = (f32[32,2,32]{2,1,0:T(2,128)S(1)}, f32[32,2,32]{2,1,0:T(2,128)S(1)}, u32[]{:S(2)}, u32[]{:S(2)}) collective-permute-start(f32[32,2,32]{2,1,0:T(2,128)S(1)} %add.39), channel_id=1, source_target_pairs={{0,128},{8,136},{16,144},{24,152},{32,160},{40,168},{48,176},{56,1... | collective-permute-start | bytes 24584 | tf_op jit(solution)/shard_map/ppermute | solution.py:52
  132.3 2.9 %collective-permute-done.4 = f32[32,2,32]{2,1,0:T(2,128)S(1)} collective-permute-done((f32[32,2,32]{2,1,0:T(2,128)S(1)}, f32[32,2,32]{2,1,0:T(2,128)S(1)}, u32[]{:S(2)}, u32[]{:S(2)}) %collective-permute-start.4) | collective-permute-done | bytes 8224 | tf_op jit(solution)/shard_map/ppermute | solution.py:52
  135.1 0.1 fusion.35
  135.2 0.2 dynamic-slice_reduce_fusion
  135.4 0.1 broadcast_in_dim.72
  135.5 0.6 select_reduce_fusion
  136.1 8.4 %fusion = f32[64,64,256]{2,0,1:T(8,128)S(1)} fusion(f32[64,64,256]{2,1,0:T(8,128)} %bitcast.18, pred[64,64]{1,0:T(32,128)(4,1)S(1)} %copy-done.10, pred[64,64]{1,0:T(32,128)(4,1)S(1)} %copy-done.9, f32[64,64]{1,0:T(8,128)S(1)} %select_reduce_fusion), kind=kOutput, calls=%fused_computation | convolution fusion | flops 805314560 | bytes 8413184 | tf_op jit(solution)/shard_map/uv,vpn->upn/dot_general | solution.py:66
  144.5 4.4 %copy.42 = f32[64,64,256]{2,1,0:T(8,128)} copy(f32[64,64,256]{2,0,1:T(8,128)S(1)} %fusion) | data formatting | bytes 8388608 | tf_op jit(solution)/shard_map/uv,vpn->upn/dot_general | solution.py:66
  148.9 9.9 %all-to-all-start.1 = ((f32[32,128,256]{2,1,0:T(8,128)}), f32[32,128,256]{2,1,0:T(8,128)}, u32[]{:S(2)}, u32[]{:S(2)}) async-start(f32[32,128,256]{2,1,0:T(8,128)} %bitcast.96), calls=%async_computation.1 | async-start | bytes 8388608 | tf_op jit(solution)/shard_map/all_to_all | solution.py:81
  158.8 0.2 convert_element_type.30
  159.1 0.2 fusion.37
  159.3 3.6 %fusion.19 = f32[2,128,1,32,64]{1,4,3,0,2:T(8,128)S(1)} fusion(f32[32,2,128]{2,0,1:T(8,128)S(1)} %copy_bitcast_fusion, f32[32,2,128]{2,0,1:T(8,128)S(1)} %reduce_window_sum.13, f32[2,128,128]{2,1,0:T(8,128)S(1)} %fusion.37, pred[128,128]{1,0:T(8,128)(4,1)S(1)} %iota_compare_fusion, bf16[2,128,32,64]{1,0,3,2:T(2,128)(2,1)} %copy-done.3), kind=kOutput, calls=%fused_computation.27 | convolution fusion | flops 139460608 | bytes 3358720 | tf_op jit(solution)/shard_map/gqkts,ksgqp->ktgqp/dot_general | solution.py:98
  162.9 1.2 fusion.36
  164.1 1.3 copy.44
  165.4 0.0 copy-start.12
  165.5 0.1 broadcast_in_dim.76
  165.5 1.3 copy.43
  166.9 0.1 broadcast_in_dim.78
  166.9 0.1 mul.87
  167.0 2.6 %copy.46 = f32[128,2048]{1,0:T(8,128)} copy(f32[128,2048]{0,1:T(8,128)} %bitcast.99) | data formatting | bytes 2097152 | tf_op jit(solution)/shard_map/squeeze | solution.py:118
  169.6 0.1 broadcast_in_dim.82
  169.7 1.3 copy.45
  171.0 0.1 select_reduce_fusion.1
  171.1 80.0 %all-to-all-done.1 = f32[32,128,256]{2,1,0:T(8,128)} async-done(((f32[32,128,256]{2,1,0:T(8,128)}), f32[32,128,256]{2,1,0:T(8,128)}, u32[]{:S(2)}, u32[]{:S(2)}) %all-to-all-start.1) | async-done | bytes 4194336 | tf_op jit(solution)/shard_map/all_to_all | solution.py:81
  251.1 1.9 slice.95
  253.0 2.2 fusion.9
  255.2 1.9 fusion.12
  257.1 0.5 fusion.8
  257.6 1.1 pad_maximum_fusion
  (39 shorter events, 0.2 us)
Async XLA Ops:
  0.0 5.3 %copy-start = (bf16[256,256]{1,0:T(8,128)(2,1)S(1)}, bf16[256,256]{1,0:T(8,128)(2,1)}, u32[]{:S(2)}) copy-start(bf16[256,256]{1,0:T(8,128)(2,1)} %param.13) | copy-start | bytes 393220
  4.2 4.0 %copy-start.3 = (bf16[2,128,32,64]{1,0,3,2:T(2,128)(2,1)}, bf16[2,128,32,64]{1,0,3,2:T(2,128)(2,1)S(1)}, u32[]{:S(2)}) copy-start(bf16[2,128,32,64]{1,0,3,2:T(2,128)(2,1)S(1)} %reshape.142) | copy-start | bytes 3145732
  8.3 127.2 %copy-start.7 = (pred[1,64,64,64]{3,2,1,0:T(32,128)(4,1)S(1)}, pred[1,64,64,64]{3,2,1,0:T(32,128)(4,1)}, u32[]{:S(2)}) copy-start(pred[1,64,64,64]{3,2,1,0:T(32,128)(4,1)} %constant.26.clone) | copy-start | bytes 786436
  8.3 127.9 %copy-start.9 = (pred[64,64]{1,0:T(32,128)(4,1)S(1)}, pred[64,64]{1,0:T(32,128)(4,1)}, u32[]{:S(2)}) copy-start(pred[64,64]{1,0:T(32,128)(4,1)} %constant.31) | copy-start | bytes 12292
  8.3 127.9 %copy-start.10 = (pred[64,64]{1,0:T(32,128)(4,1)S(1)}, pred[64,64]{1,0:T(32,128)(4,1)}, u32[]{:S(2)}) copy-start(pred[64,64]{1,0:T(32,128)(4,1)} %constant.32) | copy-start | bytes 12292
  8.3 127.8 %all-to-all-start = ((f32[32,128,256]{2,1,0:T(8,128)}), f32[32,128,256]{2,1,0:T(8,128)}, u32[]{:S(2)}, u32[]{:S(2)}) async-start(f32[32,128,256]{2,1,0:T(8,128)} %bitcast.94), calls=%async_computation | async-start | bytes 8388608 | tf_op jit(solution)/shard_map/all_to_all | solution.py:55
  19.9 91.4 %collective-permute-start = (f32[32,2,32]{2,1,0:T(2,128)S(1)}, f32[32,2,32]{2,1,0:T(2,128)S(1)}, u32[]{:S(2)}, u32[]{:S(2)}) collective-permute-start(f32[32,2,32]{2,1,0:T(2,128)S(1)} %bitcast_dynamic-update-slice_fusion), channel_id=1, source_target_pairs={{0,8},{8,0},{16,24},{24,16},{32,40},{40,32},{48,56},{56,48},{64,72... | collective-permute-start | bytes 24584 | tf_op jit(solution)/shard_map/ppermute | solution.py:52
  111.3 5.8 %collective-permute-start.1 = (f32[32,2,32]{2,1,0:T(2,128)S(1)}, f32[32,2,32]{2,1,0:T(2,128)S(1)}, u32[]{:S(2)}, u32[]{:S(2)}) collective-permute-start(f32[32,2,32]{2,1,0:T(2,128)S(1)} %fusion.32), channel_id=1, source_target_pairs={{0,16},{8,24},{16,0},{24,8},{32,48},{40,56},{48,32},{56,40},{64,80... | collective-permute-start | bytes 24584 | tf_op jit(solution)/shard_map/ppermute | solution.py:52
  117.1 7.9 %collective-permute-start.2 = (f32[32,2,32]{2,1,0:T(2,128)S(1)}, f32[32,2,32]{2,1,0:T(2,128)S(1)}, u32[]{:S(2)}, u32[]{:S(2)}) collective-permute-start(f32[32,2,32]{2,1,0:T(2,128)S(1)} %add.37), channel_id=1, source_target_pairs={{0,32},{8,40},{16,48},{24,56},{32,0},{40,8},{48,16},{56,24},{64,96... | collective-permute-start | bytes 24584 | tf_op jit(solution)/shard_map/ppermute | solution.py:52
  125.1 4.3 %collective-permute-start.3 = (f32[32,2,32]{2,1,0:T(2,128)S(1)}, f32[32,2,32]{2,1,0:T(2,128)S(1)}, u32[]{:S(2)}, u32[]{:S(2)}) collective-permute-start(f32[32,2,32]{2,1,0:T(2,128)S(1)} %add.38), channel_id=1, source_target_pairs={{0,64},{8,72},{16,80},{24,88},{32,96},{40,104},{48,112},{56,120},{... | collective-permute-start | bytes 24584 | tf_op jit(solution)/shard_map/ppermute | solution.py:52
  129.4 5.7 %collective-permute-start.4 = (f32[32,2,32]{2,1,0:T(2,128)S(1)}, f32[32,2,32]{2,1,0:T(2,128)S(1)}, u32[]{:S(2)}, u32[]{:S(2)}) collective-permute-start(f32[32,2,32]{2,1,0:T(2,128)S(1)} %add.39), channel_id=1, source_target_pairs={{0,128},{8,136},{16,144},{24,152},{32,160},{40,168},{48,176},{56,1... | collective-permute-start | bytes 24584 | tf_op jit(solution)/shard_map/ppermute | solution.py:52
  148.9 9.9 %copy-start.2 = (bf16[256,2048]{1,0:T(8,128)(2,1)S(1)}, bf16[256,2048]{1,0:T(8,128)(2,1)}, u32[]{:S(2)}) copy-start(bf16[256,2048]{1,0:T(8,128)(2,1)} %param.10) | copy-start | bytes 3145732
  148.9 10.2 %copy-start.8 = (f32[32,256]{1,0:T(8,128)S(1)}, f32[32,256]{1,0:T(8,128)}, u32[]{:S(2)}) copy-start(f32[32,256]{1,0:T(8,128)} %param.12) | copy-start | bytes 98308
  148.9 10.2 %copy-start.6 = (bf16[256,256]{1,0:T(8,128)(2,1)S(1)}, bf16[256,256]{1,0:T(8,128)(2,1)}, u32[]{:S(2)}) copy-start(bf16[256,256]{1,0:T(8,128)(2,1)} %param.14) | copy-start | bytes 393220
  148.9 102.2 %all-to-all-start.1 = ((f32[32,128,256]{2,1,0:T(8,128)}), f32[32,128,256]{2,1,0:T(8,128)}, u32[]{:S(2)}, u32[]{:S(2)}) async-start(f32[32,128,256]{2,1,0:T(8,128)} %bitcast.96), calls=%async_computation.1 | async-start | bytes 8388608 | tf_op jit(solution)/shard_map/all_to_all | solution.py:81
  162.9 4.0 %copy-start.11 = (f32[32]{0:T(128)S(1)}, f32[32]{0:T(128)}, u32[]{:S(2)}) copy-start(f32[32]{0:T(128)} %param.15) | copy-start | bytes 388
  165.4 5.5 %copy-start.12 = (s32[32,1]{0,1:T(1,128)S(1)}, s32[32,1]{0,1:T(1,128)}, u32[]{:S(2)}) copy-start(s32[32,1]{0,1:T(1,128)} %constant.29.clone) | copy-start | bytes 388
  251.1 4.1 %copy-start.1 = (f32[1,32,2,64,256]{4,3,2,1,0:T(8,128)S(1)}, f32[1,32,2,64,256]{4,3,2,1,0:T(8,128)}, u32[]{:S(2)}) copy-start(f32[1,32,2,64,256]{4,3,2,1,0:T(8,128)} %copy.40) | copy-start | bytes 12582916
  253.0 4.1 %copy-start.4 = (f32[128,2048]{1,0:T(8,128)S(1)}, f32[128,2048]{1,0:T(8,128)}, u32[]{:S(2)}) copy-start(f32[128,2048]{1,0:T(8,128)} %copy.46) | copy-start | bytes 3145732
  253.0 4.1 %copy-start.5 = (f32[128,2048]{1,0:T(8,128)S(1)}, f32[128,2048]{1,0:T(8,128)}, u32[]{:S(2)}) copy-start(f32[128,2048]{1,0:T(8,128)} %copy.45) | copy-start | bytes 3145732
